TPU v7x, 256 devices: a whole 4x4x8 slice. The times are simulated.
256 devices in a mesh: section: 16 (over z_lo, y, core), tensor: 16 (over x, z_hi).
Axes of the slice: x: 4, y: 4, z: 8 (z_hi: 4, z_lo: 2; z = z_hi * 2 + z_lo), core: 2. Of those that a mesh axis runs over, the one named last changes fastest.
Arguments:
- hidden: bfloat16 [16, 64, 8192], P('section'), may hold values from -14 to 14
- head: bfloat16 [8192, 65536], P('section', 'tensor'), may hold values from -0.25 to 0.25
- exit_loss_weight: float32 [16], P('section'), may hold values from 2 to 32
Outputs:
- grad_hidden: float32 [1024, 8192], P('tensor', 'section')
- grad_head: bfloat16 [8192, 65536], P('section', 'tensor')
All inputs are finite; a program needn't handle non-finite values.
Results may differ from a plain program's by a relative error of at most 0.011.
Values may be sent and summed in bfloat16 or wider, within the bound.
No kernel may reach another device: no remote copies, remote signals or barrier semaphores. Data moves between devices by JAX's collectives and lax.ppermute only.
A program may use at most 128 MiB of HBM per device.

v0:
```python
import jax
import jax.numpy as jnp
import numpy as np
from jax import lax
from jax.sharding import Mesh
from jax.sharding import PartitionSpec as P

scaling_divisor = 2.0
SEC = ("pair", "core")


def _lse(x, axes):
    top = jnp.max(x, axis=axes, keepdims=True)
    return top + jnp.log(jnp.sum(jnp.exp(x - top), axis=axes, keepdims=True))


def local(hidden, head, exit_loss_weight):
    pairs = lax.axis_size("pair")
    sections = pairs * 2
    tensors = lax.axis_size("tensor")
    _, tok, width = hidden.shape
    exits = sections
    dblk = width // sections
    vblk = head.shape[1]
    tps = tok // sections
    n_eq = tensors // tps
    kpe = exits // n_eq
    partner_head = lax.ppermute(head, "core", perm=[(0, 1), (1, 0)])
    head_pair = jnp.concatenate([head, partner_head], axis=0)
    h6 = hidden[0].reshape(pairs, 2, tps, pairs, 2, dblk)
    a = h6.transpose(3, 1, 0, 2, 4, 5)
    fwd = jnp.stack([a[:, 0], a[:, 1, :, :, ::-1, :]], axis=1)
    full = hidden[0].reshape(tok, sections, dblk).transpose(1, 0, 2)
    send = jnp.stack([fwd.reshape(sections, -1), full.reshape(sections, -1)], axis=1)
    recv = lax.all_to_all(send, SEC, 0, 0, tiled=True)
    cols = recv[:, 1].reshape(exits, tok, dblk)
    lhs = recv[:, 0].reshape(exits, pairs, tps, 2 * dblk).transpose(1, 0, 2, 3)
    lhs = lhs.reshape(pairs * exits * tps, 2 * dblk)
    part = jnp.dot(lhs, head_pair, preferred_element_type=jnp.float32)
    part, w_local = lax.optimization_barrier((part, exit_loss_weight))
    weights = lax.all_gather(w_local, SEC, axis=0, tiled=True)
    own = lax.psum_scatter(part, "pair", scatter_dimension=0, tiled=True)
    own, weights = lax.optimization_barrier((own, weights))
    own = own.reshape(n_eq, kpe, tps, vblk)
    stud = own.transpose(2, 0, 1, 3).reshape(tensors, kpe, vblk)
    teach = jnp.broadcast_to(own[n_eq - 1, kpe - 1][:, None, None, :], (tps, n_eq, 1, vblk))
    send2 = jnp.concatenate([stud, teach.reshape(tensors, 1, vblk)], axis=1)
    rows = lax.all_to_all(send2, "tensor", 0, 0, tiled=True)
    logits = rows[:, :kpe, :]
    teacher = rows[:, kpe, :] / scaling_divisor
    log_student = logits - _lse(logits, (0, 2))
    log_teacher = teacher - _lse(teacher, (0, 1))
    log_mixture = jnp.logaddexp(log_student, log_teacher[:, None, :]) - jnp.log(2.0)
    halfgap = 0.5 * (log_student - log_mixture)
    student = jnp.exp(log_student)
    average = jnp.sum(student * halfgap, axis=(0, 2), keepdims=True)
    eq = lax.rem(lax.axis_index("tensor"), n_eq)
    wk = lax.dynamic_slice(weights, (eq * kpe,), (kpe,))
    grad_logits = (wk[None, :, None] * student * (halfgap - average)).astype(jnp.bfloat16)
    back = lax.all_to_all(grad_logits, "tensor", 0, 0, tiled=True)
    back = back.reshape(tps, exits, vblk)
    piece = lax.all_gather(back, SEC, axis=0, tiled=True)
    head_grad = lax.dot_general(
        cols, piece, (((0, 1), (1, 0)), ((), ())), preferred_element_type=jnp.float32
    )
    row_grad = lax.dot_general(
        piece, head, (((2,), (1,)), ((), ())), preferred_element_type=jnp.float32
    )
    grad_hidden = lax.psum_scatter(row_grad, "tensor", scatter_dimension=1, tiled=True)
    grad_hidden = grad_hidden.reshape(tok, dblk)
    return (grad_hidden, head_grad.astype(jnp.bfloat16))


def solution(mesh):
    shape = mesh.devices.shape
    inner = Mesh(
        np.asarray(mesh.devices).reshape(shape[0] // 2, 2, shape[1]), ("pair", "core", "tensor")
    )
    placed = (P(SEC, None, None), P(SEC, "tensor"), P(SEC))
    return jax.shard_map(
        local,
        mesh=inner,
        in_specs=placed,
        out_specs=(P("tensor", SEC), P(SEC, "tensor")),
        check_vma=False,
    )
```

profile of v0, /device:TPU:8, one launch (start us, length us, event | category | flops | bytes accessed | tf_op | source)
XLA Modules:
  0.0 433.1 jit_solution(12043793999282986412)
XLA Ops:
  7.2 1.8 reshape_squeeze.12
  10.0 1.8 fusion.12
  11.8 2.8 rev.3
  14.5 2.5 pad_maximum_fusion.2
  19.6 3.5 copy.25
  23.1 6.3 %all-to-all-start = ((bf16[16,2,32768]{2,1,0:T(2,128)(2,1)}), bf16[16,2,32768]{2,1,0:T(2,128)(2,1)S(1)}, u32[]{:S(2)}, u32[]{:S(2)}) async-start(bf16[16,2,32768]{2,1,0:T(2,128)(2,1)} %copy.25), calls=%async_computation | async-start | bytes 4194304 | tf_op jit(solution)/shard_map/all_to_all | solution.py:35
  30.1 26.8 %all-to-all-done = bf16[16,2,32768]{2,1,0:T(2,128)(2,1)S(1)} async-done(((bf16[16,2,32768]{2,1,0:T(2,128)(2,1)}), bf16[16,2,32768]{2,1,0:T(2,128)(2,1)S(1)}, u32[]{:S(2)}, u32[]{:S(2)}) %all-to-all-start) | async-done | bytes 2097184 | tf_op jit(solution)/shard_map/all_to_all | solution.py:35
  56.9 10.0 %slice_reduce_fusion = (bf16[16,32768]{1,0:T(8,128)(2,1)S(1)}, bf16[16,32768]{1,0:T(8,128)(2,1)}) fusion(bf16[16,2,32768]{2,1,0:T(2,128)(2,1)S(1)} %all-to-all-done), kind=kLoop, calls=%fused_computation.9 | loop fusion | bytes 4194304 | tf_op jit(solution)/shard_map/slice | solution.py:36
  66.8 1.8 reshape_squeeze.14
  69.4 11.2 %fusion = f32[512,4096]{1,0:T(8,128)} fusion(bf16[512,1024]{1,0:T(8,128)(2,1)S(1)} %reshape.46, bf16[512,4096]{1,0:T(8,128)(2,1)} %collective-permute-done, bf16[512,4096]{1,0:T(8,128)(2,1)} %param.4), kind=kOutput, calls=%fused_computation | convolution fusion | flops 4311744512 | bytes 17825792 | tf_op jit(solution)/shard_map/dot_general | solution.py:39
  82.6 29.3 %all-reduce = f32[16]{0:T(128)S(1)} all-reduce(f32[16]{0:T(128)S(1)} %dynamic-update-slice), channel_id=1, replica_groups=mesh['pair'=8,'core'=2,'tensor'=16] {'pair','core'}, use_global_device_ids=true, to_apply=%add | all-reduce | flops 16 | bytes 128 | tf_op jit(solution)/shard_map/optimization_barrier | solution.py:43
  112.0 65.4 %reduce-scatter.3.cloned.1.call-done = f32[64,4096]{1,0:T(8,128)} async-done(((f32[512,4096]{1,0:T(8,128)}), f32[64,4096]{1,0:T(8,128)}) %reduce-scatter.3.cloned.1.call-update) | async-done | bytes 1048592 | tf_op jit(solution)/shard_map/reduce_scatter | solution.py:42
  177.4 1.5 reshape.47
  180.1 1.7 pad_maximum_fusion.1
  181.8 9.5 %all-to-all-start.1 = ((f32[16,5,4096]{2,1,0:T(8,128)}), f32[16,5,4096]{2,1,0:T(8,128)S(1)}, u32[]{:S(2)}, u32[]{:S(2)}) async-start(f32[16,5,4096]{2,1,0:T(8,128)} %pad_maximum_fusion.1), calls=%async_computation.2 | async-start | bytes 4194304 | tf_op jit(solution)/shard_map/all_to_all | solution.py:48
  191.6 51.3 %all-to-all-done.1 = f32[16,5,4096]{2,1,0:T(8,128)S(1)} async-done(((f32[16,5,4096]{2,1,0:T(8,128)}), f32[16,5,4096]{2,1,0:T(8,128)S(1)}, u32[]{:S(2)}, u32[]{:S(2)}) %all-to-all-start.1) | async-done | bytes 1310752 | tf_op jit(solution)/shard_map/all_to_all | solution.py:48
  244.0 1.8 exponential_reduce_fusion.1
  249.1 2.2 multiply_reduce_fusion
  251.9 22.2 %all_to_all.15 = bf16[16,4,4096]{2,1,0:T(4,128)(2,1)S(1)} all-to-all(bf16[16,4,4096]{2,1,0:T(4,128)(2,1)S(1)} %multiply_convert_fusion), channel_id=1, replica_groups=mesh['pair'=8,'core'=2,'tensor'=16] {'tensor'}, dimensions={0} | all-to-all | bytes 1048576 | tf_op jit(solution)/shard_map/all_to_all | solution.py:60
  275.1 50.5 %all-gather.2.cloned.1.call-done = bf16[64,16,4096]{2,1,0:T(8,128)(2,1)} async-done(((bf16[4,16,4096]{2,1,0:T(8,128)(2,1)}), bf16[64,16,4096]{2,1,0:T(8,128)(2,1)}) %all-gather.2.cloned.1.call-update) | async-done | bytes 8388624 | tf_op jit(solution)/shard_map/all_gather | solution.py:62
  325.6 8.2 %fusion.8 = f32[64,16,512]{2,1,0:T(8,128)S(1)} fusion(bf16[64,16,4096]{2,1,0:T(8,128)(2,1)} %all-gather.2.cloned.1.call-done, bf16[512,4096]{1,0:T(8,128)(2,1)} %param.4), kind=kOutput, calls=%fused_computation.7 | convolution fusion | flops 4294967296 | bytes 14680064 | tf_op jit(solution)/shard_map/dot_general | solution.py:66
  333.9 2.6 copy.28
  336.8 25.0 %bitcast_convert_fusion = bf16[512,4096]{1,0:T(8,128)(2,1)} fusion(bf16[16,64,512]{2,1,0:T(8,128)(2,1)S(1)} %bitcast.38, bf16[64,16,4096]{2,1,0:T(8,128)(2,1)} %all-gather.2.cloned.1.call-done), kind=kOutput, calls=%fused_computation.4 | convolution fusion | flops 4297064448 | bytes 13631488 | tf_op jit(solution)/shard_map/dot_general | solution.py:63
  361.8 64.6 %reduce-scatter.5.cloned.1.call-done = f32[64,1,512]{2,0,1:T(8,128)} async-done(((f32[64,16,512]{2,0,1:T(8,128)}), f32[64,1,512]{2,0,1:T(8,128)}) %reduce-scatter.5.cloned.1.call-update) | async-done | bytes 131088 | tf_op jit(solution)/shard_map/reduce_scatter | solution.py:69
  (37 shorter events, 12.6 us)
Async XLA Ops:
  10.0 7.9 %copy-start = (bf16[1,64,8192]{2,1,0:T(8,128)(2,1)S(1)}, bf16[1,64,8192]{2,1,0:T(8,128)(2,1)}, u32[]{:S(2)}) copy-start(bf16[1,64,8192]{2,1,0:T(8,128)(2,1)} %param.3) | copy-start | bytes 3145732
  23.1 33.8 %all-to-all-start = ((bf16[16,2,32768]{2,1,0:T(2,128)(2,1)}), bf16[16,2,32768]{2,1,0:T(2,128)(2,1)S(1)}, u32[]{:S(2)}, u32[]{:S(2)}) async-start(bf16[16,2,32768]{2,1,0:T(2,128)(2,1)} %copy.25), calls=%async_computation | async-start | bytes 4194304 | tf_op jit(solution)/shard_map/all_to_all | solution.py:35
  29.4 148.1 %reduce-scatter.3.cloned.1.call-start = ((), (), s32[]{:S(2)}) async-start(), calls=%async_computation.5 | async-start | bytes 9437184 | tf_op jit(solution)/shard_map/reduce_scatter | solution.py:42
  29.4 40.0 %collective-permute-start = (bf16[512,4096]{1,0:T(8,128)(2,1)}, bf16[512,4096]{1,0:T(8,128)(2,1)}, u32[]{:S(2)}, u32[]{:S(2)}) collective-permute-start(bf16[512,4096]{1,0:T(8,128)(2,1)} %param.4), channel_id=1, source_target_pairs={{0,16},{16,0},{1,17},{17,1},{2,18},{18,2},{3,19},{19,3},{4,20},{20... | collective-permute-start | bytes 12582920 | tf_op jit(solution)/shard_map/ppermute | solution.py:28
  80.6 0.7 copy-start.1
  181.8 61.1 %all-to-all-start.1 = ((f32[16,5,4096]{2,1,0:T(8,128)}), f32[16,5,4096]{2,1,0:T(8,128)S(1)}, u32[]{:S(2)}, u32[]{:S(2)}) async-start(f32[16,5,4096]{2,1,0:T(8,128)} %pad_maximum_fusion.1), calls=%async_computation.2 | async-start | bytes 4194304 | tf_op jit(solution)/shard_map/all_to_all | solution.py:48
  191.3 134.3 %all-gather.2.cloned.1.call-start = ((), (), s32[]{:S(2)}) async-start(), calls=%async_computation.6 | async-start | bytes 8912896 | tf_op jit(solution)/shard_map/all_gather | solution.py:62
  275.1 151.3 %reduce-scatter.5.cloned.1.call-start = ((), (), s32[]{:S(2)}) async-start(), calls=%async_computation.7 | async-start | bytes 2228224 | tf_op jit(solution)/shard_map/reduce_scatter | solution.py:69
Sparse Core Ops, SparseCore 0:
  80.8 96.6 reduce-scatter.2
  275.2 50.4 all-gather.1
  336.6 89.7 reduce-scatter.4
where the time goes:
time: 440 us; the launch traced here: 433 us
  waiting for transfers between devices  259 us (59%)
  blocking collectives  51.5 us (12%)
  matrix products  44.4 us (10%)
  local copies, waits for them, and re-layouts  33.6 us (8%)
  starting transfers between devices  16.8 us (4%)
  between operations  16.2 us (4%)
  other arithmetic  12 us (3%)
    reduce_scatter x1, waiting for transfers between devices, local(): own = lax.psum_scatter(part, 'pair', scatter_dimension=0, tiled=True)  65.4 us
    reduce_scatter x1, waiting for transfers between devices, local(): lax.psum_scatter(row_grad, 'tensor', scatter_dimension=1, tiled=True)  64.6 us
    all_to_all x1, waiting for transfers between devices, local(): rows = lax.all_to_all(send2, 'tensor', 0, 0, tiled=True)  51.3 us
    all_gather x1, waiting for transfers between devices, local(): piece = lax.all_gather(back, SEC, axis=0, tiled=True)  50.5 us
    optimization_barrier x1, blocking collectives, local(): own, weights = lax.optimization_barrier((own, weights))  29.3 us
    all_to_all x1, waiting for transfers between devices, local(): recv = lax.all_to_all(send, SEC, 0, 0, tiled=True)  26.8 us
    dot_general x1, matrix products, local(): lax.dot_general(cols, piece, (((0, 1), (1, 0)), ((), ())), preferred_elem...  25 us
    all_to_all x1, blocking collectives, local(): back = lax.all_to_all(grad_logits, 'tensor', 0, 0, tiled=True)  22.2 us
  transfers between devices with their start and end apart: 6, of which 5 were waited for; matrix products, arithmetic and copies ran while one was open for 9% of the time, Pallas kernels for 0%

commit v1 on v0

--- a/solution.py
+++ b/solution.py
@@ -59,7 +59,9 @@
     grad_logits = (wk[None, :, None] * student * (halfgap - average)).astype(jnp.bfloat16)
     back = lax.all_to_all(grad_logits, "tensor", 0, 0, tiled=True)
     back = back.reshape(tps, exits, vblk)
-    piece = lax.all_gather(back, SEC, axis=0, tiled=True)
+    piece = jnp.concatenate(
+        lax.all_to_all(jnp.stack([back] * lax.axis_size(SEC)), SEC, 0, 0), axis=0
+    )
     head_grad = lax.dot_general(
         cols, piece, (((0, 1), (1, 0)), ((), ())), preferred_element_type=jnp.float32
     )

time: 440 us -> 479 us (1.089)
  blocking collectives: 51.5 us -> 149 us
  waiting for transfers between devices: 259 us -> 203 us
    all_to_all x0 -> x1, blocking collectives: none -> 97.8 us  [local(): lax.all_to_all(jnp.stack([back] * lax.axis_size(SEC)), SEC, 0, 0)]
    all_gather x1 -> x0, waiting for transfers between devices: 50.5 us -> none  [local(): piece = lax.all_gather(back, SEC, axis=0, tiled=True)]
  transfers between devices with their start and end apart: 6 -> 5, of which waited for: 5 -> 4; matrix products, arithmetic and copies ran while one was open for 9% -> 8% of each run, Pallas kernels for 0% -> 0%
where the time goes in v1:
time: 479 us; the launch traced here: 472 us
  waiting for transfers between devices  203 us (42%)
  blocking collectives  149 us (31%)
  matrix products  40.7 us (8%)
  local copies, waits for them, and re-layouts  34.4 us (7%)
  starting transfers between devices  16.7 us (3%)
  between operations  16.5 us (3%)
  other arithmetic  10.9 us (2%)
    all_to_all x1, blocking collectives, local(): lax.all_to_all(jnp.stack([back] * lax.axis_size(SEC)), SEC, 0, 0)  97.8 us
    reduce_scatter x1, waiting for transfers between devices, local(): own = lax.psum_scatter(part, 'pair', scatter_dimension=0, tiled=True)  65.4 us
    reduce_scatter x1, waiting for transfers between devices, local(): lax.psum_scatter(row_grad, 'tensor', scatter_dimension=1, tiled=True)  59.8 us
    all_to_all x1, waiting for transfers between devices, local(): rows = lax.all_to_all(send2, 'tensor', 0, 0, tiled=True)  51.3 us
    optimization_barrier x1, blocking collectives, local(): own, weights = lax.optimization_barrier((own, weights))  29.3 us
    all_to_all x1, waiting for transfers between devices, local(): recv = lax.all_to_all(send, SEC, 0, 0, tiled=True)  26.8 us
    dot_general x1, matrix products, local(): lax.dot_general(cols, piece, (((0, 1), (1, 0)), ((), ())), preferred_elem...  25 us
    all_to_all x1, blocking collectives, local(): back = lax.all_to_all(grad_logits, 'tensor', 0, 0, tiled=True)  22.2 us
  transfers between devices with their start and end apart: 5, of which 4 were waited for; matrix products, arithmetic and copies ran while one was open for 8% of the time, Pallas kernels for 0%

profile of v1, /device:TPU:8, one launch (start us, length us, event | category | flops | bytes accessed | tf_op | source)
XLA Modules:
  0.0 471.9 jit_solution(2256680248837307044)
XLA Ops:
  7.2 1.8 reshape_squeeze.12
  9.0 1.6 copy.31
  13.7 2.8 rev.3
  16.5 1.4 pad_maximum_fusion.2
  19.0 3.5 copy.25
  22.5 6.3 %all-to-all-start = ((bf16[16,2,32768]{2,1,0:T(2,128)(2,1)}), bf16[16,2,32768]{2,1,0:T(2,128)(2,1)S(1)}, u32[]{:S(2)}, u32[]{:S(2)}) async-start(bf16[16,2,32768]{2,1,0:T(2,128)(2,1)} %copy.25), calls=%async_computation | async-start | bytes 4194304 | tf_op jit(solution)/shard_map/all_to_all | solution.py:35
  29.5 26.8 %all-to-all-done = bf16[16,2,32768]{2,1,0:T(2,128)(2,1)S(1)} async-done(((bf16[16,2,32768]{2,1,0:T(2,128)(2,1)}), bf16[16,2,32768]{2,1,0:T(2,128)(2,1)S(1)}, u32[]{:S(2)}, u32[]{:S(2)}) %all-to-all-start) | async-done | bytes 2097184 | tf_op jit(solution)/shard_map/all_to_all | solution.py:35
  56.3 10.0 %slice_reduce_fusion = (bf16[16,32768]{1,0:T(8,128)(2,1)S(1)}, bf16[16,32768]{1,0:T(8,128)(2,1)}) fusion(bf16[16,2,32768]{2,1,0:T(2,128)(2,1)S(1)} %all-to-all-done), kind=kLoop, calls=%fused_computation.9 | loop fusion | bytes 4194304 | tf_op jit(solution)/shard_map/slice | solution.py:36
  66.3 1.8 reshape_squeeze.14
  68.8 11.2 %fusion = f32[512,4096]{1,0:T(8,128)} fusion(bf16[512,1024]{1,0:T(8,128)(2,1)S(1)} %reshape.48, bf16[512,4096]{1,0:T(8,128)(2,1)} %collective-permute-done, bf16[512,4096]{1,0:T(8,128)(2,1)} %param.4), kind=kOutput, calls=%fused_computation | convolution fusion | flops 4311744512 | bytes 17825792 | tf_op jit(solution)/shard_map/dot_general | solution.py:39
  82.1 29.3 %all-reduce = f32[16]{0:T(128)S(1)} all-reduce(f32[16]{0:T(128)S(1)} %dynamic-update-slice), channel_id=1, replica_groups=mesh['pair'=8,'core'=2,'tensor'=16] {'pair','core'}, use_global_device_ids=true, to_apply=%add | all-reduce | flops 16 | bytes 128 | tf_op jit(solution)/shard_map/optimization_barrier | solution.py:43
  111.4 65.4 %reduce-scatter.3.cloned.1.call-done = f32[64,4096]{1,0:T(8,128)} async-done(((f32[512,4096]{1,0:T(8,128)}), f32[64,4096]{1,0:T(8,128)}) %reduce-scatter.3.cloned.1.call-update) | async-done | bytes 1048592 | tf_op jit(solution)/shard_map/reduce_scatter | solution.py:42
  176.9 1.5 reshape.49
  179.5 1.7 pad_maximum_fusion.1
  181.2 9.5 %all-to-all-start.1 = ((f32[16,5,4096]{2,1,0:T(8,128)}), f32[16,5,4096]{2,1,0:T(8,128)S(1)}, u32[]{:S(2)}, u32[]{:S(2)}) async-start(f32[16,5,4096]{2,1,0:T(8,128)} %pad_maximum_fusion.1), calls=%async_computation.2 | async-start | bytes 4194304 | tf_op jit(solution)/shard_map/all_to_all | solution.py:48
  191.1 51.3 %all-to-all-done.1 = f32[16,5,4096]{2,1,0:T(8,128)S(1)} async-done(((f32[16,5,4096]{2,1,0:T(8,128)}), f32[16,5,4096]{2,1,0:T(8,128)S(1)}, u32[]{:S(2)}, u32[]{:S(2)}) %all-to-all-start.1) | async-done | bytes 1310752 | tf_op jit(solution)/shard_map/all_to_all | solution.py:48
  243.5 1.8 exponential_reduce_fusion.1
  248.5 2.2 multiply_reduce_fusion
  251.4 22.2 %all_to_all.20 = bf16[16,4,4096]{2,1,0:T(4,128)(2,1)S(1)} all-to-all(bf16[16,4,4096]{2,1,0:T(4,128)(2,1)S(1)} %multiply_convert_fusion), channel_id=1, replica_groups=mesh['pair'=8,'core'=2,'tensor'=16] {'tensor'}, dimensions={0} | all-to-all | bytes 1048576 | tf_op jit(solution)/shard_map/all_to_all | solution.py:60
  274.7 97.8 %all_to_all.21 = bf16[16,4,16,4096]{3,2,1,0:T(8,128)(2,1)S(1)} all-to-all(bf16[16,4,16,4096]{3,2,1,0:T(8,128)(2,1)S(1)} %stack.11), channel_id=1, replica_groups=mesh['pair'=8,'core'=2,'tensor'=16] {'pair','core'}, dimensions={0} | all-to-all | bytes 16777216 | tf_op jit(solution)/shard_map/all_to_all | solution.py:63
  372.5 4.5 fusion.8
  377.1 2.6 copy.28
  380.0 25.0 %bitcast_convert_fusion = bf16[512,4096]{1,0:T(8,128)(2,1)} fusion(bf16[16,64,512]{2,1,0:T(8,128)(2,1)S(1)} %bitcast.41, bf16[64,16,4096]{2,1,0:T(8,128)(2,1)} %bitcast.32), kind=kOutput, calls=%fused_computation.4 | convolution fusion | flops 4297064448 | bytes 13631488 | tf_op jit(solution)/shard_map/dot_general | solution.py:65
  405.0 59.8 %reduce-scatter.5.cloned.1.call-done = f32[64,1,512]{2,0,1:T(8,128)} async-done(((f32[64,16,512]{2,0,1:T(8,128)}), f32[64,1,512]{2,0,1:T(8,128)}) %reduce-scatter.5.cloned.1.call-update) | async-done | bytes 131088 | tf_op jit(solution)/shard_map/reduce_scatter | solution.py:71
  (38 shorter events, 13.5 us)
Async XLA Ops:
  22.5 33.8 %all-to-all-start = ((bf16[16,2,32768]{2,1,0:T(2,128)(2,1)}), bf16[16,2,32768]{2,1,0:T(2,128)(2,1)S(1)}, u32[]{:S(2)}, u32[]{:S(2)}) async-start(bf16[16,2,32768]{2,1,0:T(2,128)(2,1)} %copy.25), calls=%async_computation | async-start | bytes 4194304 | tf_op jit(solution)/shard_map/all_to_all | solution.py:35
  28.8 148.1 %reduce-scatter.3.cloned.1.call-start = ((), (), s32[]{:S(2)}) async-start(), calls=%async_computation.6 | async-start | bytes 9437184 | tf_op jit(solution)/shard_map/reduce_scatter | solution.py:42
  28.8 40.0 %collective-permute-start = (bf16[512,4096]{1,0:T(8,128)(2,1)}, bf16[512,4096]{1,0:T(8,128)(2,1)}, u32[]{:S(2)}, u32[]{:S(2)}) collective-permute-start(bf16[512,4096]{1,0:T(8,128)(2,1)} %param.4), channel_id=1, source_target_pairs={{0,16},{16,0},{1,17},{17,1},{2,18},{18,2},{3,19},{19,3},{4,20},{20... | collective-permute-start | bytes 12582920 | tf_op jit(solution)/shard_map/ppermute | solution.py:28
  80.0 0.7 copy-start.2
  181.2 61.1 %all-to-all-start.1 = ((f32[16,5,4096]{2,1,0:T(8,128)}), f32[16,5,4096]{2,1,0:T(8,128)S(1)}, u32[]{:S(2)}, u32[]{:S(2)}) async-start(f32[16,5,4096]{2,1,0:T(8,128)} %pad_maximum_fusion.1), calls=%async_computation.2 | async-start | bytes 4194304 | tf_op jit(solution)/shard_map/all_to_all | solution.py:48
  190.8 274.1 %reduce-scatter.5.cloned.1.call-start = ((), (), s32[]{:S(2)}) async-start(), calls=%async_computation.7 | async-start | bytes 2228224 | tf_op jit(solution)/shard_map/reduce_scatter | solution.py:71
  274.7 97.8 %copy-start.1 = (bf16[512,4096]{1,0:T(8,128)(2,1)S(1)}, bf16[512,4096]{1,0:T(8,128)(2,1)}, u32[]{:S(2)}) copy-start(bf16[512,4096]{1,0:T(8,128)(2,1)} %param.4) | copy-start | bytes 12582916
  372.5 4.5 copy-start
Sparse Core Ops, SparseCore 0:
  80.2 96.6 reduce-scatter.2
  379.8 85.0 reduce-scatter.4
